TPU v7x, 256 devices: a whole 4x4x8 slice. The times are simulated.
256 devices in a mesh: sec: 16 (over x, y), vel: 16 (over z, core).
Axes of the slice: x: 4, y: 4, z: 8, core: 2. Of those that a mesh axis runs over, the one named last changes fastest.
Arguments:
- distribution: float32 [13824, 4096], P('vel', 'sec'), may hold values from -6 to 6
- collision: float32 [4096], P('sec'), may hold values from 0.05 to 2
- lower_blocks: float32 [25, 4096], P(None, 'sec'), may hold values from -0.6 to 0.6
- upper_blocks: float32 [25, 4096], P(None, 'sec'), may hold values from -0.6 to 0.6
- diag_inverse: float32 [25, 4096], P(None, 'sec'), may hold values from -0.2 to 1.4
Outputs:
- new_distribution: float32 [13824, 4096], P('vel', 'sec')
- macro: float32 [5, 4096], P(None, 'sec')
All inputs are finite; a program needn't handle non-finite values.
Results may differ from a plain program's by a relative error of at most 0.0003.
Values sent between devices are 32-bit elements; how exact they have to be, the bound alone decides.
No kernel may reach another device: no remote copies, remote signals or barrier semaphores. Data moves between devices by JAX's collectives and lax.ppermute only.
A program may use at most 64 MiB of HBM per device.

v0:
```python
import math
import jax
import jax.numpy as jnp
import numpy as np
from jax import lax
from jax.sharding import PartitionSpec as P

NXI = 24
TUBES = 128
JACOBI = 4
NEWTON = 2
HIGH = lax.Precision.HIGHEST
pseudo_rate = 1.0


def passed_along(block, axis, distance):
    devices = range(lax.axis_size(axis))
    route = [(i - distance, i) for i in devices if i - distance in devices]
    return lax.ppermute(block, axis, route)


def extended(array, sides, width):
    for axis, dim in sides:
        count, length = (lax.axis_size(axis), array.shape[dim])
        up = [(i, (i + 1) % count) for i in range(count - 1)]
        down = [(j, i) for i, j in up]
        last = lax.slice_in_dim(array, length - width, length, axis=dim)
        first = lax.slice_in_dim(array, 0, width, axis=dim)
        before = lax.ppermute(last, axis, up)
        after = lax.ppermute(first, axis, down)
        array = jnp.concatenate([before, array, after], axis=dim)
    return array


def hermite_rule(count):
    quarter = math.pi ** (-0.25)
    found = []
    last_slope = 1.0
    for index in range(count // 2):
        if index == 0:
            guess = math.sqrt(2.0 * count + 1.0) - 1.85575 * (2.0 * count + 1.0) ** (-0.16667)
        elif index == 1:
            guess = guess - 1.14 * count**0.426 / guess
        elif index == 2:
            guess = 1.86 * guess - 0.86 * found[0][0]
        elif index == 3:
            guess = 1.91 * guess - 0.91 * found[1][0]
        else:
            guess = 2.0 * guess - found[index - 2][0]
        for repeat in range(60):
            current = quarter
            previous = 0.0
            for order in range(count):
                older = previous
                previous = current
                current = (
                    guess * math.sqrt(2.0 / (order + 1)) * previous
                    - math.sqrt(order / (order + 1.0)) * older
                )
            last_slope = math.sqrt(2.0 * count) * previous
            guess = guess - current / last_slope
        found.append((guess, 2.0 / (last_slope * last_slope)))
    positive = found[::-1]
    points = [-pair[0] for pair in found] + [pair[0] for pair in positive]
    weights = [pair[1] for pair in found] + [pair[1] for pair in positive]
    return (np.array(points), np.array(weights))


def node_tables(axis_points):
    points, weights = hermite_rule(axis_points)
    node_index = np.arange(axis_points**3)
    idx_x = node_index % axis_points
    idx_z = node_index // axis_points % axis_points
    idx_y = node_index // (axis_points * axis_points)
    along_x = points[idx_x]
    along_y = points[idx_y]
    along_z = points[idx_z]
    node_weight = weights[idx_x] * weights[idx_y] * weights[idx_z] / math.pi**1.5
    energy = along_x**2 + along_y**2 + along_z**2 - 1.5
    moment_basis = np.stack([along_x * 0.0 + 1.0, along_x, along_y, along_z, energy])
    norm_scale = np.array([1.0, 0.5, 0.5, 0.5, 1.5])
    return (
        along_x,
        node_weight,
        moment_basis * node_weight[None, :],
        moment_basis / norm_scale[:, None],
    )


def apply_block(matrices, vector):
    shaped = matrices.reshape((5, 5) + vector.shape[1:])
    return jnp.sum(shaped * vector[None], axis=1)


def affine_combine(earlier_map, later_map):
    return (later_map[0] * earlier_map[0], later_map[0] * earlier_map[1] + later_map[1])


def newton_sums(loaded, signed, shift_mass, shift_flow):
    growth = jnp.exp(shift_mass + shift_flow * signed)
    scaled = loaded * growth
    excess = loaded * (growth - 1.0)
    return jnp.stack(
        [
            jnp.sum(scaled),
            jnp.sum(scaled * signed),
            jnp.sum(scaled * signed * signed),
            jnp.sum(excess),
            jnp.sum(excess * signed),
        ]
    )


def newton_update(shift_mass, shift_flow, sums, goal_mass, goal_flow):
    resid_mass = sums[3] - goal_mass
    resid_flow = sums[4] - goal_flow
    determinant = sums[0] * sums[2] - sums[1] * sums[1]
    new_mass = shift_mass - (sums[2] * resid_mass - sums[1] * resid_flow) / determinant
    new_flow = shift_flow - (sums[0] * resid_flow - sums[1] * resid_mass) / determinant
    return (new_mass, new_flow)


def received(block, distance):
    count = lax.axis_size("sec")
    if abs(distance) >= count:
        return jnp.zeros_like(block)
    return passed_along(block, "sec", distance)


def exclusive_inflow(rate, drive, sign):
    count = lax.axis_size("sec")

    def fetch(a, b, distance):
        got = received(jnp.concatenate([a, b], axis=0), sign * distance)
        return (got[:1], got[1:])

    near_a, near_b = fetch(rate, drive, 1)
    span = 1
    if count > 2:
        far_a, far_b = fetch(rate, drive, 2)
        near_a, near_b = (near_a * far_a, near_a * far_b + near_b)
        span = 2
    while span < count - 1:
        got_a, got_b = fetch(near_a, near_b, span)
        near_a, near_b = (near_a * got_a, near_a * got_b + near_b)
        span *= 2
    return near_b


def with_halo(array, width):
    parts = [received(array, d) for d in range(width, 0, -1)]
    parts.append(array)
    parts.extend((received(array, -d) for d in range(1, width + 1)))
    return jnp.concatenate(parts, axis=1)


def body(distribution, collision, lower_blocks, upper_blocks, diag_inverse):
    node_count = distribution.shape[0]
    cell_count = distribution.shape[1]
    length = cell_count // TUBES
    node_rows = node_count // NXI
    half_nodes = NXI // 2
    along_x, node_weight, weighted_np, rebuild_np = node_tables(NXI)
    all_mass = jnp.asarray(node_weight, jnp.float32)
    offset = lax.axis_index("vel") * node_count
    weighted = lax.dynamic_slice_in_dim(
        jnp.asarray(weighted_np, jnp.float32), offset, node_count, 1
    )
    rebuild = lax.dynamic_slice_in_dim(jnp.asarray(rebuild_np, jnp.float32), offset, node_count, 1)
    node_mass = lax.dynamic_slice_in_dim(all_mass, offset, node_count, 0)
    line_signed = jnp.asarray(along_x[:NXI], jnp.float32)
    old_moments = lax.psum(jnp.dot(weighted, distribution, precision=HIGH), "vel")
    target = jnp.dot(rebuild.T, old_moments, precision=HIGH)
    total_length = length * lax.axis_size("sec")
    thickness = collision.reshape(1, 1, length, TUBES)
    node_speed = jnp.abs(line_signed).reshape(1, NXI, 1, 1)
    denominator = node_speed * total_length + thickness + pseudo_rate
    carry_rate = node_speed * total_length / denominator
    drive_term = (
        thickness * target.reshape(node_rows, NXI, length, TUBES)
        + pseudo_rate * distribution.reshape(node_rows, NXI, length, TUBES)
    ) / denominator
    prod_neg, local_neg = lax.associative_scan(
        affine_combine,
        (
            jnp.broadcast_to(carry_rate[:, :half_nodes], (1, half_nodes, length, TUBES)),
            drive_term[:, :half_nodes],
        ),
        reverse=True,
        axis=2,
    )
    prod_pos, local_pos = lax.associative_scan(
        affine_combine,
        (
            jnp.broadcast_to(carry_rate[:, half_nodes:], (1, NXI - half_nodes, length, TUBES)),
            drive_term[:, half_nodes:],
        ),
        axis=2,
    )
    inflow_pos = exclusive_inflow(prod_pos[:, :, -1], local_pos[:, :, -1], 1)
    inflow_neg = exclusive_inflow(prod_neg[:, :, 0], local_neg[:, :, 0], -1)
    field_neg = local_neg + prod_neg * inflow_neg[:, :, None, :]
    field_pos = local_pos + prod_pos * inflow_pos[:, :, None, :]
    half_field = jnp.concatenate([field_neg, field_pos], axis=1).reshape(node_count, cell_count)
    half_moments = lax.psum(jnp.dot(weighted, half_field, precision=HIGH), "vel")
    residual = (half_moments - old_moments).reshape(5, length, TUBES)
    width = min(-(-JACOBI // length), lax.axis_size("sec") - 1)
    blocks = jnp.concatenate([lower_blocks, upper_blocks, diag_inverse], axis=0)
    blocks_wide = with_halo(blocks.reshape(75, length, TUBES), width)
    lower_r = blocks_wide[:25]
    upper_r = blocks_wide[25:50]
    inverse_r = blocks_wide[50:]
    residual_wide = with_halo(residual, width)
    correction = apply_block(inverse_r, residual_wide)
    edge_zero = jnp.zeros((5, 1, TUBES), jnp.float32)
    for sweep_index in range(JACOBI):
        from_left = jnp.concatenate([edge_zero, correction[:, :-1]], axis=1)
        from_right = jnp.concatenate([correction[:, 1:], edge_zero], axis=1)
        correction = apply_block(
            inverse_r,
            residual_wide - apply_block(lower_r, from_left) - apply_block(upper_r, from_right),
        )
    correction = correction[:, width * length : (width + 1) * length].reshape(5, cell_count)
    macro = half_moments + correction
    synthetic = half_field + jnp.dot(rebuild.T, correction, precision=HIGH)
    local_totals = jnp.sum(old_moments - macro, axis=1)[0:2]
    magnitude = jnp.sum(jnp.abs(synthetic), axis=1)
    line_loaded = jnp.sum((node_mass * magnitude).reshape(node_rows, NXI), axis=0)
    first_copy = (lax.axis_index("vel") == 0).astype(jnp.float32)
    gathered = lax.psum(jnp.concatenate([line_loaded, local_totals * first_copy]), ("sec", "vel"))
    loaded = gathered[:NXI]
    goals = gathered[NXI:]
    shift_mass = jnp.zeros((), jnp.float32)
    shift_flow = jnp.zeros((), jnp.float32)
    for newton_turn in range(NEWTON):
        sums = newton_sums(loaded, line_signed, shift_mass, shift_flow)
        shift_mass, shift_flow = newton_update(shift_mass, shift_flow, sums, goals[0], goals[1])
    growth = jnp.exp(shift_mass + shift_flow * line_signed)
    synthetic_rows = synthetic.reshape(node_rows, NXI, cell_count)
    new_distribution = synthetic_rows + jnp.abs(synthetic_rows) * (growth[None, :, None] - 1.0)
    return (new_distribution.reshape(node_count, cell_count), macro)


def solution(mesh):
    in_specs = (P("vel", "sec"), P("sec"), P(None, "sec"), P(None, "sec"), P(None, "sec"))
    out_specs = (P("vel", "sec"), P(None, "sec"))
    return jax.shard_map(body, mesh=mesh, in_specs=in_specs, out_specs=out_specs, check_vma=False)
```

profile of v0, /device:TPU:1, one launch (start us, length us, event | category | flops | bytes accessed | tf_op | source)
XLA Modules:
  0.0 254.2 jit_solution(769121284347335400)
XLA Ops:
  0.7 0.7 copy-done.4
  1.5 1.7 reshape.255
  3.2 1.3 fusion.13
  4.5 27.9 %psum.21 = f32[5,256]{1,0:T(8,128)S(1)} all-reduce(f32[5,256]{1,0:T(8,128)S(1)} %fusion.13), channel_id=1, replica_groups=mesh['sec'=16,'vel'=16] {'vel'}, use_global_device_ids=true, to_apply=%region_0.0 | all-reduce | flops 1280 | bytes 10240 | tf_op jit(solution)/shard_map/psum | solution.py:172
  32.4 1.8 fusion.16
  34.3 0.5 reshape.254
  34.9 0.7 fusion.29
  36.0 1.3 collective-permute-start
  37.4 1.3 collective-permute-start.1
  38.8 6.2 %collective-permute-start.10 = (f32[75,2,128]{2,1,0:T(2,128)S(1)}, f32[75,2,128]{2,1,0:T(2,128)S(1)}, u32[]{:S(2)}, u32[]{:S(2)}) collective-permute-start(f32[75,2,128]{2,1,0:T(2,128)S(1)} %reshape.257), channel_id=1, source_target_pairs={{0,32},{16,48},{32,64},{48,80},{64,96},{80,112},{96,128},{112,144}... | collective-permute-start | bytes 230408 | tf_op jit(solution)/shard_map/ppermute | solution.py:19
  45.0 3.2 %collective-permute-start.11 = (f32[75,2,128]{2,1,0:T(2,128)S(1)}, f32[75,2,128]{2,1,0:T(2,128)S(1)}, u32[]{:S(2)}, u32[]{:S(2)}) collective-permute-start(f32[75,2,128]{2,1,0:T(2,128)S(1)} %reshape.257), channel_id=1, source_target_pairs={{0,16},{16,32},{32,48},{48,64},{64,80},{80,96},{96,112},{112,128},... | collective-permute-start | bytes 230408 | tf_op jit(solution)/shard_map/ppermute | solution.py:19
  48.3 1.3 collective-permute-start.12
  49.9 1.1 rev.8
  51.1 0.4 fusion.11
  51.6 1.3 collective-permute-start.13
  52.9 4.7 %collective-permute-start.5 = (f32[37,12,128]{2,0,1:T(8,128)S(1)}, f32[37,12,128]{2,0,1:T(8,128)S(1)}, u32[]{:S(2)}, u32[]{:S(2)}) collective-permute-start(f32[37,12,128]{2,0,1:T(8,128)S(1)} %pad_maximum_fusion.5), channel_id=1, source_target_pairs={{0,16},{16,32},{32,48},{48,64},{64,80},{80,96},{96,112},{112,128},... | collective-permute-start | bytes 681992 | tf_op jit(solution)/shard_map/ppermute | solution.py:19
  57.6 6.8 %collective-permute-start.6 = (f32[37,12,128]{2,0,1:T(8,128)S(1)}, f32[37,12,128]{2,0,1:T(8,128)S(1)}, u32[]{:S(2)}, u32[]{:S(2)}) collective-permute-start(f32[37,12,128]{2,0,1:T(8,128)S(1)} %pad_maximum_fusion.5), channel_id=1, source_target_pairs={{0,32},{16,48},{32,64},{48,80},{64,96},{80,112},{96,128},{112,144}... | collective-permute-start | bytes 681992 | tf_op jit(solution)/shard_map/ppermute | solution.py:19
  64.4 2.1 concatenate.91
  66.7 1.3 collective-permute-start.2
  68.0 0.7 collective-permute-done.6
  68.8 5.4 %collective-permute-start.7 = (f32[37,12,128]{2,0,1:T(8,128)S(1)}, f32[37,12,128]{2,0,1:T(8,128)S(1)}, u32[]{:S(2)}, u32[]{:S(2)}) collective-permute-start(f32[37,12,128]{2,0,1:T(8,128)S(1)} %pad_maximum_fusion.6), channel_id=1, source_target_pairs={{0,32},{16,48},{32,64},{48,80},{64,96},{80,112},{96,128},{112,144}... | collective-permute-start | bytes 681992 | tf_op jit(solution)/shard_map/ppermute | solution.py:19
  74.3 1.2 collective-permute-done.2
  75.5 1.3 collective-permute-start.3
  76.8 4.3 %collective-permute-done.7 = f32[37,12,128]{2,0,1:T(8,128)S(1)} collective-permute-done((f32[37,12,128]{2,0,1:T(8,128)S(1)}, f32[37,12,128]{2,0,1:T(8,128)S(1)}, u32[]{:S(2)}, u32[]{:S(2)}) %collective-permute-start.7) | collective-permute-done | bytes 227360 | tf_op jit(solution)/shard_map/ppermute | solution.py:19
  81.3 8.1 %collective-permute-start.8 = (f32[37,12,128]{2,0,1:T(8,128)S(1)}, f32[37,12,128]{2,0,1:T(8,128)S(1)}, u32[]{:S(2)}, u32[]{:S(2)}) collective-permute-start(f32[37,12,128]{2,0,1:T(8,128)S(1)} %pad_maximum_fusion.7), channel_id=1, source_target_pairs={{0,64},{16,80},{32,96},{48,112},{64,128},{80,144},{96,160},{112,17... | collective-permute-start | bytes 681992 | tf_op jit(solution)/shard_map/ppermute | solution.py:19
  89.4 1.5 collective-permute-done.3
  91.0 1.3 collective-permute-start.4
  92.6 5.9 %collective-permute-start.9 = (f32[37,12,128]{2,0,1:T(8,128)S(1)}, f32[37,12,128]{2,0,1:T(8,128)S(1)}, u32[]{:S(2)}, u32[]{:S(2)}) collective-permute-start(f32[37,12,128]{2,0,1:T(8,128)S(1)} %pad_maximum_fusion.8), channel_id=1, source_target_pairs={{0,128},{16,144},{32,160},{48,176},{64,192},{80,208},{96,224},{112... | collective-permute-start | bytes 681992 | tf_op jit(solution)/shard_map/ppermute | solution.py:19
  98.5 0.9 collective-permute-done.4
  99.5 2.8 %collective-permute-done.9 = f32[37,12,128]{2,0,1:T(8,128)S(1)} collective-permute-done((f32[37,12,128]{2,0,1:T(8,128)S(1)}, f32[37,12,128]{2,0,1:T(8,128)S(1)}, u32[]{:S(2)}, u32[]{:S(2)}) %collective-permute-start.9) | collective-permute-done | bytes 227360 | tf_op jit(solution)/shard_map/ppermute | solution.py:19
  102.4 0.5 fusion.3
  103.1 0.4 pad_maximum_fusion
  103.5 1.3 fusion
  104.8 36.0 %psum.22 = f32[5,256]{1,0:T(8,128)S(1)} all-reduce(f32[5,256]{1,0:T(8,128)S(1)} %fusion), channel_id=1, replica_groups=mesh['sec'=16,'vel'=16] {'vel'}, use_global_device_ids=true, to_apply=%region_1.0 | all-reduce | flops 1280 | bytes 10240 | tf_op jit(solution)/shard_map/psum | solution.py:205
  140.8 2.7 %collective-permute-start.14 = (f32[5,2,128]{2,1,0:T(2,128)S(1)}, f32[5,2,128]{2,1,0:T(2,128)S(1)}, u32[]{:S(2)}, u32[]{:S(2)}) collective-permute-start(f32[5,2,128]{2,1,0:T(2,128)S(1)} %reshape.259), channel_id=1, source_target_pairs={{0,32},{16,48},{32,64},{48,80},{64,96},{80,112},{96,128},{112,144}... | collective-permute-start | bytes 15368 | tf_op jit(solution)/shard_map/ppermute | solution.py:19
  143.6 1.3 collective-permute-start.15
  144.9 1.3 collective-permute-start.16
  146.2 1.3 collective-permute-start.17
  147.5 1.7 collective-permute-done.16
  149.2 2.9 %collective-permute-done.17 = f32[5,2,128]{2,1,0:T(2,128)S(1)} collective-permute-done((f32[5,2,128]{2,1,0:T(2,128)S(1)}, f32[5,2,128]{2,1,0:T(2,128)S(1)}, u32[]{:S(2)}, u32[]{:S(2)}) %collective-permute-start.17) | collective-permute-done | bytes 5152 | tf_op jit(solution)/shard_map/ppermute | solution.py:19
  152.8 1.9 abs_reduce_fusion
  154.8 0.7 subtract_reduce_fusion
  155.5 0.8 dynamic-slice_multiply_fusion
  156.4 79.3 %psum.23 = f32[26]{0:T(128)S(1)} all-reduce(f32[26]{0:T(128)S(1)} %pad_maximum_fusion.10), channel_id=1, replica_groups=mesh['sec'=16,'vel'=16] {'sec','vel'}, use_global_device_ids=true, to_apply=%region_18.0 | all-reduce | flops 26 | bytes 208 | tf_op jit(solution)/shard_map/psum | solution.py:230
  235.8 0.7 fusion.36
  236.5 0.7 multiply_reduce_fusion.14
  244.7 0.7 multiply_reduce_fusion.13
  253.1 1.1 multiply_add_fusion
  (116 shorter events, 3.3 us)
Async XLA Ops:
  0.6 0.7 copy-start.4
  0.6 0.7 copy-start.6
  1.5 1.7 copy-start
  36.0 2.7 %copy-start.1 = (f32[25,256]{1,0:T(8,128)S(1)}, f32[25,256]{1,0:T(8,128)}, u32[]{:S(2)}) copy-start(f32[25,256]{1,0:T(8,128)} %param.13) | copy-start | bytes 76804
  36.0 2.7 %copy-start.2 = (f32[25,256]{1,0:T(8,128)S(1)}, f32[25,256]{1,0:T(8,128)}, u32[]{:S(2)}) copy-start(f32[25,256]{1,0:T(8,128)} %param.12) | copy-start | bytes 76804
  36.0 2.7 %copy-start.3 = (f32[25,256]{1,0:T(8,128)S(1)}, f32[25,256]{1,0:T(8,128)}, u32[]{:S(2)}) copy-start(f32[25,256]{1,0:T(8,128)} %param.11) | copy-start | bytes 76804
  36.0 30.5 %collective-permute-start = (f32[37,12,128]{2,0,1:T(8,128)S(1)}, f32[37,12,128]{2,0,1:T(8,128)S(1)}, u32[]{:S(2)}, u32[]{:S(2)}) collective-permute-start(f32[37,12,128]{2,0,1:T(8,128)S(1)} %pad_maximum_fusion.1), channel_id=1, source_target_pairs={{16,0},{32,16},{48,32},{64,48},{80,64},{96,80},{112,96},{128,112},... | collective-permute-start | bytes 681992 | tf_op jit(solution)/shard_map/ppermute | solution.py:19
  37.4 29.2 %collective-permute-start.1 = (f32[37,12,128]{2,0,1:T(8,128)S(1)}, f32[37,12,128]{2,0,1:T(8,128)S(1)}, u32[]{:S(2)}, u32[]{:S(2)}) collective-permute-start(f32[37,12,128]{2,0,1:T(8,128)S(1)} %pad_maximum_fusion.1), channel_id=1, source_target_pairs={{32,0},{48,16},{64,32},{80,48},{96,64},{112,80},{128,96},{144,112}... | collective-permute-start | bytes 681992 | tf_op jit(solution)/shard_map/ppermute | solution.py:19
  38.8 12.8 %collective-permute-start.10 = (f32[75,2,128]{2,1,0:T(2,128)S(1)}, f32[75,2,128]{2,1,0:T(2,128)S(1)}, u32[]{:S(2)}, u32[]{:S(2)}) collective-permute-start(f32[75,2,128]{2,1,0:T(2,128)S(1)} %reshape.257), channel_id=1, source_target_pairs={{0,32},{16,48},{32,64},{48,80},{64,96},{80,112},{96,128},{112,144}... | collective-permute-start | bytes 230408 | tf_op jit(solution)/shard_map/ppermute | solution.py:19
  45.0 7.9 %collective-permute-start.11 = (f32[75,2,128]{2,1,0:T(2,128)S(1)}, f32[75,2,128]{2,1,0:T(2,128)S(1)}, u32[]{:S(2)}, u32[]{:S(2)}) collective-permute-start(f32[75,2,128]{2,1,0:T(2,128)S(1)} %reshape.257), channel_id=1, source_target_pairs={{0,16},{16,32},{32,48},{48,64},{64,80},{80,96},{96,112},{112,128},... | collective-permute-start | bytes 230408 | tf_op jit(solution)/shard_map/ppermute | solution.py:19
  48.3 9.4 %collective-permute-start.12 = (f32[75,2,128]{2,1,0:T(2,128)S(1)}, f32[75,2,128]{2,1,0:T(2,128)S(1)}, u32[]{:S(2)}, u32[]{:S(2)}) collective-permute-start(f32[75,2,128]{2,1,0:T(2,128)S(1)} %reshape.257), channel_id=1, source_target_pairs={{16,0},{32,16},{48,32},{64,48},{80,64},{96,80},{112,96},{128,112},... | collective-permute-start | bytes 230408 | tf_op jit(solution)/shard_map/ppermute | solution.py:19
  51.6 12.9 %collective-permute-start.13 = (f32[75,2,128]{2,1,0:T(2,128)S(1)}, f32[75,2,128]{2,1,0:T(2,128)S(1)}, u32[]{:S(2)}, u32[]{:S(2)}) collective-permute-start(f32[75,2,128]{2,1,0:T(2,128)S(1)} %reshape.257), channel_id=1, source_target_pairs={{32,0},{48,16},{64,32},{80,48},{96,64},{112,80},{128,96},{144,112}... | collective-permute-start | bytes 230408 | tf_op jit(solution)/shard_map/ppermute | solution.py:19
  52.9 15.1 %collective-permute-start.5 = (f32[37,12,128]{2,0,1:T(8,128)S(1)}, f32[37,12,128]{2,0,1:T(8,128)S(1)}, u32[]{:S(2)}, u32[]{:S(2)}) collective-permute-start(f32[37,12,128]{2,0,1:T(8,128)S(1)} %pad_maximum_fusion.5), channel_id=1, source_target_pairs={{0,16},{16,32},{32,48},{48,64},{64,80},{80,96},{96,112},{112,128},... | collective-permute-start | bytes 681992 | tf_op jit(solution)/shard_map/ppermute | solution.py:19
  57.6 11.1 %collective-permute-start.6 = (f32[37,12,128]{2,0,1:T(8,128)S(1)}, f32[37,12,128]{2,0,1:T(8,128)S(1)}, u32[]{:S(2)}, u32[]{:S(2)}) collective-permute-start(f32[37,12,128]{2,0,1:T(8,128)S(1)} %pad_maximum_fusion.5), channel_id=1, source_target_pairs={{0,32},{16,48},{32,64},{48,80},{64,96},{80,112},{96,128},{112,144}... | collective-permute-start | bytes 681992 | tf_op jit(solution)/shard_map/ppermute | solution.py:19
  66.7 8.7 %collective-permute-start.2 = (f32[37,12,128]{2,0,1:T(8,128)S(1)}, f32[37,12,128]{2,0,1:T(8,128)S(1)}, u32[]{:S(2)}, u32[]{:S(2)}) collective-permute-start(f32[37,12,128]{2,0,1:T(8,128)S(1)} %pad_maximum_fusion.2), channel_id=1, source_target_pairs={{32,0},{48,16},{64,32},{80,48},{96,64},{112,80},{128,96},{144,112}... | collective-permute-start | bytes 681992 | tf_op jit(solution)/shard_map/ppermute | solution.py:19
  68.8 12.3 %collective-permute-start.7 = (f32[37,12,128]{2,0,1:T(8,128)S(1)}, f32[37,12,128]{2,0,1:T(8,128)S(1)}, u32[]{:S(2)}, u32[]{:S(2)}) collective-permute-start(f32[37,12,128]{2,0,1:T(8,128)S(1)} %pad_maximum_fusion.6), channel_id=1, source_target_pairs={{0,32},{16,48},{32,64},{48,80},{64,96},{80,112},{96,128},{112,144}... | collective-permute-start | bytes 681992 | tf_op jit(solution)/shard_map/ppermute | solution.py:19
  75.5 15.4 %collective-permute-start.3 = (f32[37,12,128]{2,0,1:T(8,128)S(1)}, f32[37,12,128]{2,0,1:T(8,128)S(1)}, u32[]{:S(2)}, u32[]{:S(2)}) collective-permute-start(f32[37,12,128]{2,0,1:T(8,128)S(1)} %pad_maximum_fusion.3), channel_id=1, source_target_pairs={{64,0},{80,16},{96,32},{112,48},{128,64},{144,80},{160,96},{176,11... | collective-permute-start | bytes 681992 | tf_op jit(solution)/shard_map/ppermute | solution.py:19
  81.3 11.2 %collective-permute-start.8 = (f32[37,12,128]{2,0,1:T(8,128)S(1)}, f32[37,12,128]{2,0,1:T(8,128)S(1)}, u32[]{:S(2)}, u32[]{:S(2)}) collective-permute-start(f32[37,12,128]{2,0,1:T(8,128)S(1)} %pad_maximum_fusion.7), channel_id=1, source_target_pairs={{0,64},{16,80},{32,96},{48,112},{64,128},{80,144},{96,160},{112,17... | collective-permute-start | bytes 681992 | tf_op jit(solution)/shard_map/ppermute | solution.py:19
  91.0 8.4 %collective-permute-start.4 = (f32[37,12,128]{2,0,1:T(8,128)S(1)}, f32[37,12,128]{2,0,1:T(8,128)S(1)}, u32[]{:S(2)}, u32[]{:S(2)}) collective-permute-start(f32[37,12,128]{2,0,1:T(8,128)S(1)} %pad_maximum_fusion.4), channel_id=1, source_target_pairs={{128,0},{144,16},{160,32},{176,48},{192,64},{208,80},{224,96},{240... | collective-permute-start | bytes 681992 | tf_op jit(solution)/shard_map/ppermute | solution.py:19
  92.6 9.7 %collective-permute-start.9 = (f32[37,12,128]{2,0,1:T(8,128)S(1)}, f32[37,12,128]{2,0,1:T(8,128)S(1)}, u32[]{:S(2)}, u32[]{:S(2)}) collective-permute-start(f32[37,12,128]{2,0,1:T(8,128)S(1)} %pad_maximum_fusion.8), channel_id=1, source_target_pairs={{0,128},{16,144},{32,160},{48,176},{64,192},{80,208},{96,224},{112... | collective-permute-start | bytes 681992 | tf_op jit(solution)/shard_map/ppermute | solution.py:19
  140.8 6.7 %collective-permute-start.14 = (f32[5,2,128]{2,1,0:T(2,128)S(1)}, f32[5,2,128]{2,1,0:T(2,128)S(1)}, u32[]{:S(2)}, u32[]{:S(2)}) collective-permute-start(f32[5,2,128]{2,1,0:T(2,128)S(1)} %reshape.259), channel_id=1, source_target_pairs={{0,32},{16,48},{32,64},{48,80},{64,96},{80,112},{96,128},{112,144}... | collective-permute-start | bytes 15368 | tf_op jit(solution)/shard_map/ppermute | solution.py:19
  143.6 4.0 %collective-permute-start.15 = (f32[5,2,128]{2,1,0:T(2,128)S(1)}, f32[5,2,128]{2,1,0:T(2,128)S(1)}, u32[]{:S(2)}, u32[]{:S(2)}) collective-permute-start(f32[5,2,128]{2,1,0:T(2,128)S(1)} %reshape.259), channel_id=1, source_target_pairs={{0,16},{16,32},{32,48},{48,64},{64,80},{80,96},{96,112},{112,128},... | collective-permute-start | bytes 15368 | tf_op jit(solution)/shard_map/ppermute | solution.py:19
  144.9 4.4 %collective-permute-start.16 = (f32[5,2,128]{2,1,0:T(2,128)S(1)}, f32[5,2,128]{2,1,0:T(2,128)S(1)}, u32[]{:S(2)}, u32[]{:S(2)}) collective-permute-start(f32[5,2,128]{2,1,0:T(2,128)S(1)} %reshape.259), channel_id=1, source_target_pairs={{16,0},{32,16},{48,32},{64,48},{80,64},{96,80},{112,96},{128,112},... | collective-permute-start | bytes 15368 | tf_op jit(solution)/shard_map/ppermute | solution.py:19
  146.2 6.0 %collective-permute-start.17 = (f32[5,2,128]{2,1,0:T(2,128)S(1)}, f32[5,2,128]{2,1,0:T(2,128)S(1)}, u32[]{:S(2)}, u32[]{:S(2)}) collective-permute-start(f32[5,2,128]{2,1,0:T(2,128)S(1)} %reshape.259), channel_id=1, source_target_pairs={{32,0},{48,16},{64,32},{80,48},{96,64},{112,80},{128,96},{144,112}... | collective-permute-start | bytes 15368 | tf_op jit(solution)/shard_map/ppermute | solution.py:19
  235.8 0.7 copy-start.5
  235.8 0.7 copy-start.7
where the time goes:
time: 255 us; the launch traced here: 254 us
  blocking collectives  143 us (56%)
  starting transfers between devices  56.1 us (22%)
  between operations  16.8 us (7%)
  waiting for transfers between devices  16.2 us (6%)
  other arithmetic  8.25 us (3%)
  local copies, waits for them, and re-layouts  7.31 us (3%)
  matrix products  6.31 us (2%)
    psum x1, blocking collectives, body(): lax.psum(jnp.concatenate([line_loaded, local_totals * first_copy]), ('sec...  79.3 us
    ppermute x18, starting transfers between devices, passed_along(): return lax.ppermute(block, axis, route)  56.1 us
    psum x1, blocking collectives, body(): lax.psum(jnp.dot(weighted, half_field, precision=HIGH), 'vel')  36 us
    psum x1, blocking collectives, body(): lax.psum(jnp.dot(weighted, distribution, precision=HIGH), 'vel')  27.9 us
    ppermute x18, waiting for transfers between devices, passed_along(): return lax.ppermute(block, axis, route)  16.2 us
  transfers between devices with their start and end apart: 18, of which 9 were waited for; matrix products, arithmetic and copies ran while one was open for 2% of the time, Pallas kernels for 0%

commit v1 on v0

--- a/solution.py
+++ b/solution.py
@@ -227,7 +227,10 @@
     magnitude = jnp.sum(jnp.abs(synthetic), axis=1)
     line_loaded = jnp.sum((node_mass * magnitude).reshape(node_rows, NXI), axis=0)
     first_copy = (lax.axis_index("vel") == 0).astype(jnp.float32)
-    gathered = lax.psum(jnp.concatenate([line_loaded, local_totals * first_copy]), ("sec", "vel"))
+    gathered = lax.psum(
+        lax.psum(jnp.concatenate([line_loaded, local_totals * first_copy]), axis_name="sec"),
+        axis_name="vel",
+    )
     loaded = gathered[:NXI]
     goals = gathered[NXI:]
     shift_mass = jnp.zeros((), jnp.float32)

time: 255 us -> 239 us (0.937)
  blocking collectives: 143 us -> 127 us
    psum x1 -> x2, blocking collectives: 79.3 us -> 63 us  [the longest x1 31.8 us: body(): lax.psum(lax.psum(jnp.concatenate([line_loaded, local_totals * first_copy...]
where the time goes in v1:
time: 239 us; the launch traced here: 238 us
  blocking collectives  127 us (53%)
  starting transfers between devices  56.1 us (23%)
  between operations  16.8 us (7%)
  waiting for transfers between devices  16.2 us (7%)
  other arithmetic  8.25 us (3%)
  local copies, waits for them, and re-layouts  7.31 us (3%)
  matrix products  6.31 us (3%)
    ppermute x18, starting transfers between devices, passed_along(): return lax.ppermute(block, axis, route)  56.1 us
    psum x1, blocking collectives, body(): lax.psum(jnp.dot(weighted, half_field, precision=HIGH), 'vel')  36 us
    psum x1, blocking collectives, body(): lax.psum(lax.psum(jnp.concatenate([line_loaded, local_totals * first_copy...  31.8 us
    psum x1, blocking collectives, body(): lax.psum(jnp.concatenate([line_loaded, local_totals * first_copy]), axis_...  31.2 us
    psum x1, blocking collectives, body(): lax.psum(jnp.dot(weighted, distribution, precision=HIGH), 'vel')  27.9 us
    ppermute x18, waiting for transfers between devices, passed_along(): return lax.ppermute(block, axis, route)  16.2 us
  transfers between devices with their start and end apart: 18, of which 9 were waited for; matrix products, arithmetic and copies ran while one was open for 2% of the time, Pallas kernels for 0%

profile of v1, /device:TPU:1, one launch (start us, length us, event | category | flops | bytes accessed | tf_op | source)
XLA Modules:
  0.0 237.8 jit_solution(10836248660838269395)
XLA Ops:
  0.7 0.7 copy-done.4
  1.5 1.7 reshape.255
  3.2 1.3 fusion.13
  4.5 27.9 %psum.28 = f32[5,256]{1,0:T(8,128)S(1)} all-reduce(f32[5,256]{1,0:T(8,128)S(1)} %fusion.13), channel_id=1, replica_groups=mesh['sec'=16,'vel'=16] {'vel'}, use_global_device_ids=true, to_apply=%region_0.0 | all-reduce | flops 1280 | bytes 10240 | tf_op jit(solution)/shard_map/psum | solution.py:172
  32.4 1.8 fusion.16
  34.3 0.5 reshape.254
  34.9 0.7 fusion.29
  36.0 1.3 collective-permute-start
  37.4 1.3 collective-permute-start.1
  38.8 6.2 %collective-permute-start.10 = (f32[75,2,128]{2,1,0:T(2,128)S(1)}, f32[75,2,128]{2,1,0:T(2,128)S(1)}, u32[]{:S(2)}, u32[]{:S(2)}) collective-permute-start(f32[75,2,128]{2,1,0:T(2,128)S(1)} %reshape.257), channel_id=1, source_target_pairs={{0,32},{16,48},{32,64},{48,80},{64,96},{80,112},{96,128},{112,144}... | collective-permute-start | bytes 230408 | tf_op jit(solution)/shard_map/ppermute | solution.py:19
  45.0 3.2 %collective-permute-start.11 = (f32[75,2,128]{2,1,0:T(2,128)S(1)}, f32[75,2,128]{2,1,0:T(2,128)S(1)}, u32[]{:S(2)}, u32[]{:S(2)}) collective-permute-start(f32[75,2,128]{2,1,0:T(2,128)S(1)} %reshape.257), channel_id=1, source_target_pairs={{0,16},{16,32},{32,48},{48,64},{64,80},{80,96},{96,112},{112,128},... | collective-permute-start | bytes 230408 | tf_op jit(solution)/shard_map/ppermute | solution.py:19
  48.3 1.3 collective-permute-start.12
  49.9 1.1 rev.8
  51.6 1.3 collective-permute-start.13
  52.9 4.7 %collective-permute-start.5 = (f32[37,12,128]{2,0,1:T(8,128)S(1)}, f32[37,12,128]{2,0,1:T(8,128)S(1)}, u32[]{:S(2)}, u32[]{:S(2)}) collective-permute-start(f32[37,12,128]{2,0,1:T(8,128)S(1)} %pad_maximum_fusion.5), channel_id=1, source_target_pairs={{0,16},{16,32},{32,48},{48,64},{64,80},{80,96},{96,112},{112,128},... | collective-permute-start | bytes 681992 | tf_op jit(solution)/shard_map/ppermute | solution.py:19
  57.6 6.8 %collective-permute-start.6 = (f32[37,12,128]{2,0,1:T(8,128)S(1)}, f32[37,12,128]{2,0,1:T(8,128)S(1)}, u32[]{:S(2)}, u32[]{:S(2)}) collective-permute-start(f32[37,12,128]{2,0,1:T(8,128)S(1)} %pad_maximum_fusion.5), channel_id=1, source_target_pairs={{0,32},{16,48},{32,64},{48,80},{64,96},{80,112},{96,128},{112,144}... | collective-permute-start | bytes 681992 | tf_op jit(solution)/shard_map/ppermute | solution.py:19
  64.4 2.1 concatenate.91
  66.7 1.3 collective-permute-start.2
  68.0 0.7 collective-permute-done.6
  68.8 5.4 %collective-permute-start.7 = (f32[37,12,128]{2,0,1:T(8,128)S(1)}, f32[37,12,128]{2,0,1:T(8,128)S(1)}, u32[]{:S(2)}, u32[]{:S(2)}) collective-permute-start(f32[37,12,128]{2,0,1:T(8,128)S(1)} %pad_maximum_fusion.6), channel_id=1, source_target_pairs={{0,32},{16,48},{32,64},{48,80},{64,96},{80,112},{96,128},{112,144}... | collective-permute-start | bytes 681992 | tf_op jit(solution)/shard_map/ppermute | solution.py:19
  74.3 1.2 collective-permute-done.2
  75.5 1.3 collective-permute-start.3
  76.8 4.3 %collective-permute-done.7 = f32[37,12,128]{2,0,1:T(8,128)S(1)} collective-permute-done((f32[37,12,128]{2,0,1:T(8,128)S(1)}, f32[37,12,128]{2,0,1:T(8,128)S(1)}, u32[]{:S(2)}, u32[]{:S(2)}) %collective-permute-start.7) | collective-permute-done | bytes 227360 | tf_op jit(solution)/shard_map/ppermute | solution.py:19
  81.3 8.1 %collective-permute-start.8 = (f32[37,12,128]{2,0,1:T(8,128)S(1)}, f32[37,12,128]{2,0,1:T(8,128)S(1)}, u32[]{:S(2)}, u32[]{:S(2)}) collective-permute-start(f32[37,12,128]{2,0,1:T(8,128)S(1)} %pad_maximum_fusion.7), channel_id=1, source_target_pairs={{0,64},{16,80},{32,96},{48,112},{64,128},{80,144},{96,160},{112,17... | collective-permute-start | bytes 681992 | tf_op jit(solution)/shard_map/ppermute | solution.py:19
  89.4 1.5 collective-permute-done.3
  91.0 1.3 collective-permute-start.4
  92.6 5.9 %collective-permute-start.9 = (f32[37,12,128]{2,0,1:T(8,128)S(1)}, f32[37,12,128]{2,0,1:T(8,128)S(1)}, u32[]{:S(2)}, u32[]{:S(2)}) collective-permute-start(f32[37,12,128]{2,0,1:T(8,128)S(1)} %pad_maximum_fusion.8), channel_id=1, source_target_pairs={{0,128},{16,144},{32,160},{48,176},{64,192},{80,208},{96,224},{112... | collective-permute-start | bytes 681992 | tf_op jit(solution)/shard_map/ppermute | solution.py:19
  98.5 0.9 collective-permute-done.4
  99.5 2.8 %collective-permute-done.9 = f32[37,12,128]{2,0,1:T(8,128)S(1)} collective-permute-done((f32[37,12,128]{2,0,1:T(8,128)S(1)}, f32[37,12,128]{2,0,1:T(8,128)S(1)}, u32[]{:S(2)}, u32[]{:S(2)}) %collective-permute-start.9) | collective-permute-done | bytes 227360 | tf_op jit(solution)/shard_map/ppermute | solution.py:19
  102.4 0.5 fusion.3
  103.1 0.4 pad_maximum_fusion
  103.5 1.3 fusion
  104.8 36.0 %psum.29 = f32[5,256]{1,0:T(8,128)S(1)} all-reduce(f32[5,256]{1,0:T(8,128)S(1)} %fusion), channel_id=1, replica_groups=mesh['sec'=16,'vel'=16] {'vel'}, use_global_device_ids=true, to_apply=%region_1.0 | all-reduce | flops 1280 | bytes 10240 | tf_op jit(solution)/shard_map/psum | solution.py:205
  140.8 2.7 %collective-permute-start.14 = (f32[5,2,128]{2,1,0:T(2,128)S(1)}, f32[5,2,128]{2,1,0:T(2,128)S(1)}, u32[]{:S(2)}, u32[]{:S(2)}) collective-permute-start(f32[5,2,128]{2,1,0:T(2,128)S(1)} %reshape.259), channel_id=1, source_target_pairs={{0,32},{16,48},{32,64},{48,80},{64,96},{80,112},{96,128},{112,144}... | collective-permute-start | bytes 15368 | tf_op jit(solution)/shard_map/ppermute | solution.py:19
  143.6 1.3 collective-permute-start.15
  144.9 1.3 collective-permute-start.16
  146.2 1.3 collective-permute-start.17
  147.5 1.7 collective-permute-done.16
  149.2 2.9 %collective-permute-done.17 = f32[5,2,128]{2,1,0:T(2,128)S(1)} collective-permute-done((f32[5,2,128]{2,1,0:T(2,128)S(1)}, f32[5,2,128]{2,1,0:T(2,128)S(1)}, u32[]{:S(2)}, u32[]{:S(2)}) %collective-permute-start.17) | collective-permute-done | bytes 5152 | tf_op jit(solution)/shard_map/ppermute | solution.py:19
  152.8 1.9 abs_reduce_fusion
  154.8 0.7 subtract_reduce_fusion
  155.5 0.8 dynamic-slice_multiply_fusion
  156.4 31.2 %psum.30 = f32[26]{0:T(128)S(1)} all-reduce(f32[26]{0:T(128)S(1)} %pad_maximum_fusion.10), channel_id=1, replica_groups=mesh['sec'=16,'vel'=16] {'sec'}, use_global_device_ids=true, to_apply=%region_18.0 | all-reduce | flops 26 | bytes 208 | tf_op jit(solution)/shard_map/psum | solution.py:231
  187.6 31.8 %psum.31 = f32[26]{0:T(128)S(1)} all-reduce(f32[26]{0:T(128)S(1)} %psum.30), channel_id=1, replica_groups=mesh['sec'=16,'vel'=16] {'vel'}, use_global_device_ids=true, to_apply=%region_19.0 | all-reduce | flops 26 | bytes 208 | tf_op jit(solution)/shard_map/psum | solution.py:230
  219.4 0.7 fusion.36
  220.1 0.7 multiply_reduce_fusion.14
  228.3 0.7 multiply_reduce_fusion.13
  236.7 1.1 multiply_add_fusion
  (117 shorter events, 3.7 us)
Async XLA Ops:
  0.6 0.7 copy-start.4
  0.6 0.7 copy-start.6
  1.5 1.7 copy-start
  36.0 2.7 %copy-start.1 = (f32[25,256]{1,0:T(8,128)S(1)}, f32[25,256]{1,0:T(8,128)}, u32[]{:S(2)}) copy-start(f32[25,256]{1,0:T(8,128)} %param.13) | copy-start | bytes 76804
  36.0 2.7 %copy-start.2 = (f32[25,256]{1,0:T(8,128)S(1)}, f32[25,256]{1,0:T(8,128)}, u32[]{:S(2)}) copy-start(f32[25,256]{1,0:T(8,128)} %param.12) | copy-start | bytes 76804
  36.0 2.7 %copy-start.3 = (f32[25,256]{1,0:T(8,128)S(1)}, f32[25,256]{1,0:T(8,128)}, u32[]{:S(2)}) copy-start(f32[25,256]{1,0:T(8,128)} %param.11) | copy-start | bytes 76804
  36.0 30.5 %collective-permute-start = (f32[37,12,128]{2,0,1:T(8,128)S(1)}, f32[37,12,128]{2,0,1:T(8,128)S(1)}, u32[]{:S(2)}, u32[]{:S(2)}) collective-permute-start(f32[37,12,128]{2,0,1:T(8,128)S(1)} %pad_maximum_fusion.1), channel_id=1, source_target_pairs={{16,0},{32,16},{48,32},{64,48},{80,64},{96,80},{112,96},{128,112},... | collective-permute-start | bytes 681992 | tf_op jit(solution)/shard_map/ppermute | solution.py:19
  37.4 29.2 %collective-permute-start.1 = (f32[37,12,128]{2,0,1:T(8,128)S(1)}, f32[37,12,128]{2,0,1:T(8,128)S(1)}, u32[]{:S(2)}, u32[]{:S(2)}) collective-permute-start(f32[37,12,128]{2,0,1:T(8,128)S(1)} %pad_maximum_fusion.1), channel_id=1, source_target_pairs={{32,0},{48,16},{64,32},{80,48},{96,64},{112,80},{128,96},{144,112}... | collective-permute-start | bytes 681992 | tf_op jit(solution)/shard_map/ppermute | solution.py:19
  38.8 12.8 %collective-permute-start.10 = (f32[75,2,128]{2,1,0:T(2,128)S(1)}, f32[75,2,128]{2,1,0:T(2,128)S(1)}, u32[]{:S(2)}, u32[]{:S(2)}) collective-permute-start(f32[75,2,128]{2,1,0:T(2,128)S(1)} %reshape.257), channel_id=1, source_target_pairs={{0,32},{16,48},{32,64},{48,80},{64,96},{80,112},{96,128},{112,144}... | collective-permute-start | bytes 230408 | tf_op jit(solution)/shard_map/ppermute | solution.py:19
  45.0 7.9 %collective-permute-start.11 = (f32[75,2,128]{2,1,0:T(2,128)S(1)}, f32[75,2,128]{2,1,0:T(2,128)S(1)}, u32[]{:S(2)}, u32[]{:S(2)}) collective-permute-start(f32[75,2,128]{2,1,0:T(2,128)S(1)} %reshape.257), channel_id=1, source_target_pairs={{0,16},{16,32},{32,48},{48,64},{64,80},{80,96},{96,112},{112,128},... | collective-permute-start | bytes 230408 | tf_op jit(solution)/shard_map/ppermute | solution.py:19
  48.3 9.4 %collective-permute-start.12 = (f32[75,2,128]{2,1,0:T(2,128)S(1)}, f32[75,2,128]{2,1,0:T(2,128)S(1)}, u32[]{:S(2)}, u32[]{:S(2)}) collective-permute-start(f32[75,2,128]{2,1,0:T(2,128)S(1)} %reshape.257), channel_id=1, source_target_pairs={{16,0},{32,16},{48,32},{64,48},{80,64},{96,80},{112,96},{128,112},... | collective-permute-start | bytes 230408 | tf_op jit(solution)/shard_map/ppermute | solution.py:19
  51.6 12.9 %collective-permute-start.13 = (f32[75,2,128]{2,1,0:T(2,128)S(1)}, f32[75,2,128]{2,1,0:T(2,128)S(1)}, u32[]{:S(2)}, u32[]{:S(2)}) collective-permute-start(f32[75,2,128]{2,1,0:T(2,128)S(1)} %reshape.257), channel_id=1, source_target_pairs={{32,0},{48,16},{64,32},{80,48},{96,64},{112,80},{128,96},{144,112}... | collective-permute-start | bytes 230408 | tf_op jit(solution)/shard_map/ppermute | solution.py:19
  52.9 15.1 %collective-permute-start.5 = (f32[37,12,128]{2,0,1:T(8,128)S(1)}, f32[37,12,128]{2,0,1:T(8,128)S(1)}, u32[]{:S(2)}, u32[]{:S(2)}) collective-permute-start(f32[37,12,128]{2,0,1:T(8,128)S(1)} %pad_maximum_fusion.5), channel_id=1, source_target_pairs={{0,16},{16,32},{32,48},{48,64},{64,80},{80,96},{96,112},{112,128},... | collective-permute-start | bytes 681992 | tf_op jit(solution)/shard_map/ppermute | solution.py:19
  57.6 11.1 %collective-permute-start.6 = (f32[37,12,128]{2,0,1:T(8,128)S(1)}, f32[37,12,128]{2,0,1:T(8,128)S(1)}, u32[]{:S(2)}, u32[]{:S(2)}) collective-permute-start(f32[37,12,128]{2,0,1:T(8,128)S(1)} %pad_maximum_fusion.5), channel_id=1, source_target_pairs={{0,32},{16,48},{32,64},{48,80},{64,96},{80,112},{96,128},{112,144}... | collective-permute-start | bytes 681992 | tf_op jit(solution)/shard_map/ppermute | solution.py:19
  66.7 8.7 %collective-permute-start.2 = (f32[37,12,128]{2,0,1:T(8,128)S(1)}, f32[37,12,128]{2,0,1:T(8,128)S(1)}, u32[]{:S(2)}, u32[]{:S(2)}) collective-permute-start(f32[37,12,128]{2,0,1:T(8,128)S(1)} %pad_maximum_fusion.2), channel_id=1, source_target_pairs={{32,0},{48,16},{64,32},{80,48},{96,64},{112,80},{128,96},{144,112}... | collective-permute-start | bytes 681992 | tf_op jit(solution)/shard_map/ppermute | solution.py:19
  68.8 12.3 %collective-permute-start.7 = (f32[37,12,128]{2,0,1:T(8,128)S(1)}, f32[37,12,128]{2,0,1:T(8,128)S(1)}, u32[]{:S(2)}, u32[]{:S(2)}) collective-permute-start(f32[37,12,128]{2,0,1:T(8,128)S(1)} %pad_maximum_fusion.6), channel_id=1, source_target_pairs={{0,32},{16,48},{32,64},{48,80},{64,96},{80,112},{96,128},{112,144}... | collective-permute-start | bytes 681992 | tf_op jit(solution)/shard_map/ppermute | solution.py:19
  75.5 15.4 %collective-permute-start.3 = (f32[37,12,128]{2,0,1:T(8,128)S(1)}, f32[37,12,128]{2,0,1:T(8,128)S(1)}, u32[]{:S(2)}, u32[]{:S(2)}) collective-permute-start(f32[37,12,128]{2,0,1:T(8,128)S(1)} %pad_maximum_fusion.3), channel_id=1, source_target_pairs={{64,0},{80,16},{96,32},{112,48},{128,64},{144,80},{160,96},{176,11... | collective-permute-start | bytes 681992 | tf_op jit(solution)/shard_map/ppermute | solution.py:19
  81.3 11.2 %collective-permute-start.8 = (f32[37,12,128]{2,0,1:T(8,128)S(1)}, f32[37,12,128]{2,0,1:T(8,128)S(1)}, u32[]{:S(2)}, u32[]{:S(2)}) collective-permute-start(f32[37,12,128]{2,0,1:T(8,128)S(1)} %pad_maximum_fusion.7), channel_id=1, source_target_pairs={{0,64},{16,80},{32,96},{48,112},{64,128},{80,144},{96,160},{112,17... | collective-permute-start | bytes 681992 | tf_op jit(solution)/shard_map/ppermute | solution.py:19
  91.0 8.4 %collective-permute-start.4 = (f32[37,12,128]{2,0,1:T(8,128)S(1)}, f32[37,12,128]{2,0,1:T(8,128)S(1)}, u32[]{:S(2)}, u32[]{:S(2)}) collective-permute-start(f32[37,12,128]{2,0,1:T(8,128)S(1)} %pad_maximum_fusion.4), channel_id=1, source_target_pairs={{128,0},{144,16},{160,32},{176,48},{192,64},{208,80},{224,96},{240... | collective-permute-start | bytes 681992 | tf_op jit(solution)/shard_map/ppermute | solution.py:19
  92.6 9.7 %collective-permute-start.9 = (f32[37,12,128]{2,0,1:T(8,128)S(1)}, f32[37,12,128]{2,0,1:T(8,128)S(1)}, u32[]{:S(2)}, u32[]{:S(2)}) collective-permute-start(f32[37,12,128]{2,0,1:T(8,128)S(1)} %pad_maximum_fusion.8), channel_id=1, source_target_pairs={{0,128},{16,144},{32,160},{48,176},{64,192},{80,208},{96,224},{112... | collective-permute-start | bytes 681992 | tf_op jit(solution)/shard_map/ppermute | solution.py:19
  140.8 6.7 %collective-permute-start.14 = (f32[5,2,128]{2,1,0:T(2,128)S(1)}, f32[5,2,128]{2,1,0:T(2,128)S(1)}, u32[]{:S(2)}, u32[]{:S(2)}) collective-permute-start(f32[5,2,128]{2,1,0:T(2,128)S(1)} %reshape.259), channel_id=1, source_target_pairs={{0,32},{16,48},{32,64},{48,80},{64,96},{80,112},{96,128},{112,144}... | collective-permute-start | bytes 15368 | tf_op jit(solution)/shard_map/ppermute | solution.py:19
  143.6 4.0 %collective-permute-start.15 = (f32[5,2,128]{2,1,0:T(2,128)S(1)}, f32[5,2,128]{2,1,0:T(2,128)S(1)}, u32[]{:S(2)}, u32[]{:S(2)}) collective-permute-start(f32[5,2,128]{2,1,0:T(2,128)S(1)} %reshape.259), channel_id=1, source_target_pairs={{0,16},{16,32},{32,48},{48,64},{64,80},{80,96},{96,112},{112,128},... | collective-permute-start | bytes 15368 | tf_op jit(solution)/shard_map/ppermute | solution.py:19
  144.9 4.4 %collective-permute-start.16 = (f32[5,2,128]{2,1,0:T(2,128)S(1)}, f32[5,2,128]{2,1,0:T(2,128)S(1)}, u32[]{:S(2)}, u32[]{:S(2)}) collective-permute-start(f32[5,2,128]{2,1,0:T(2,128)S(1)} %reshape.259), channel_id=1, source_target_pairs={{16,0},{32,16},{48,32},{64,48},{80,64},{96,80},{112,96},{128,112},... | collective-permute-start | bytes 15368 | tf_op jit(solution)/shard_map/ppermute | solution.py:19
  146.2 6.0 %collective-permute-start.17 = (f32[5,2,128]{2,1,0:T(2,128)S(1)}, f32[5,2,128]{2,1,0:T(2,128)S(1)}, u32[]{:S(2)}, u32[]{:S(2)}) collective-permute-start(f32[5,2,128]{2,1,0:T(2,128)S(1)} %reshape.259), channel_id=1, source_target_pairs={{32,0},{48,16},{64,32},{80,48},{96,64},{112,80},{128,96},{144,112}... | collective-permute-start | bytes 15368 | tf_op jit(solution)/shard_map/ppermute | solution.py:19
  219.4 0.7 copy-start.5
  219.4 0.7 copy-start.7
